TPU v7x, 512 devices: a whole 4x4x16 slice. The times are simulated.
512 devices in a mesh: section: 32 (over z_hi, y, core), tp: 16 (over z_lo, x).
Axes of the slice: x: 4, y: 4, z: 16 (z_hi: 4, z_lo: 4; z = z_hi * 4 + z_lo), core: 2. Of those that a mesh axis runs over, the one named last changes fastest.
Arguments:
- grad_in: bfloat16 [32, 160, 8192], P('section', None, 'tp'), may hold values from -6 to 6
- out_proj: bfloat16 [32, 4096, 8192], P('section', 'tp'), may hold values from -0.09375 to 0.09375
- value_proj: bfloat16 [32, 8192, 512], P('section', 'tp'), may hold values from -0.0625 to 0.0625
- head_delta: bfloat16 [32, 160, 4096], P('section', None, 'tp'), may hold values from -6 to 6
- pattern: bfloat16 [32, 32, 160, 160], P('section', 'tp'), may hold values from 0 to 0.25
- positions: int32 [160], replicated, may hold values from -1 to 31, as said below
- node_map: int32 [32, 32], P('section'), may hold values from 0 to 31, each once within a row
Outputs:
- residual_grad: bfloat16 [32, 160, 8192], P('section', None, 'tp')
- edge_scores: float32 [32, 32, 32], P('section')
Inputs may be any that keep to these rules, and one draw needn't show every extreme that they name: positions[t] = (t mod 32) - p, or -1 where that is negative, with one left padding p of 0 to 15 for each block of 32 tokens; the first block is unpadded. `node_map`: each row names every node once.
All inputs are finite; a program needn't handle non-finite values.
Results may differ from a plain program's by a relative error of at most 0.0095.
Values may be sent and summed in bfloat16 or wider, within the bound.
No kernel may reach another device: no remote copies, remote signals or barrier semaphores. Data moves between devices by JAX's collectives and lax.ppermute only.
A program may use at most 128 MiB of HBM per device.

v0:
```python
import jax
import jax.numpy as jnp
from jax import lax
from jax.sharding import PartitionSpec as P

HEADS = 32
HEAD_DIM = 128
KV = 4
PROMPT = 32
GROUP = 8


def on_device(grad_in, out_proj, value_proj, head_delta, pattern, positions, node_map):
    tokens = grad_in.shape[1]
    local_width = grad_in.shape[2]
    own_rows = out_proj.shape[1]
    own_heads = own_rows // HEAD_DIM
    width = out_proj.shape[2]
    tp_count = lax.axis_size("tp")
    section_count = lax.axis_size("section")
    weights = out_proj[0]
    blocks = weights.reshape(own_rows, tp_count, width // tp_count).transpose(1, 0, 2)
    column_blocks = lax.all_to_all(blocks, "tp", 0, 0, tiled=True)
    all_delta_cols = lax.all_gather(head_delta[0], "tp", axis=1, tiled=True)
    token_ids = jnp.arange(tokens)
    block_ids = token_ids // PROMPT
    allowed = (
        (block_ids[:, None] == block_ids[None, :])
        & (positions[None, :] >= 0)
        & (positions[None, :] <= positions[:, None])
    )
    visible = allowed.astype(jnp.bfloat16)
    grad_rows = lax.all_gather(grad_in[0], "tp", axis=1, tiled=True)
    head_grad = lax.dot_general(
        grad_rows, weights, (((1,), (1,)), ((), ())), preferred_element_type=jnp.float32
    ).astype(jnp.bfloat16)
    masked = pattern[0] * visible[None]
    value_grad = jnp.einsum(
        "hts,thc->shc",
        masked,
        head_grad.reshape(tokens, own_heads, HEAD_DIM),
        preferred_element_type=jnp.float32,
    ).astype(jnp.bfloat16)
    pair_sum = value_grad.astype(jnp.float32).sum(axis=1)
    group_of = lax.axis_index("tp") * own_heads // GROUP
    slots = jnp.zeros((tokens, KV, HEAD_DIM), jnp.float32)
    slots = lax.dynamic_update_slice(slots, pair_sum[:, None, :], (0, group_of, 0))
    summed = lax.psum(slots, "tp")
    group_grad = summed.reshape(tokens, KV * HEAD_DIM).astype(jnp.bfloat16)
    increment = lax.dot_general(
        group_grad, value_proj[0], (((1,), (1,)), ((), ())), preferred_element_type=jnp.float32
    )
    residual_grad = (grad_in[0].astype(jnp.float32) + increment).astype(jnp.bfloat16)
    target_row = increment.astype(jnp.bfloat16)
    target_rows = lax.all_gather(target_row[None], "section", axis=0, tiled=True)
    delta = jnp.einsum(
        "thc,hcd->htd",
        all_delta_cols.reshape(tokens, HEADS, HEAD_DIM),
        column_blocks.reshape(HEADS, HEAD_DIM, local_width),
        preferred_element_type=jnp.float32,
    ).astype(jnp.bfloat16)
    partial_scores = lax.dot_general(
        delta.reshape(HEADS, tokens * local_width),
        target_rows.reshape(section_count, tokens * local_width),
        (((1,), (1,)), ((), ())),
        preferred_element_type=jnp.float32,
    )
    totals = lax.psum(partial_scores, "tp")
    later = jnp.arange(section_count) > lax.axis_index("section")
    raw_scores = jnp.where(later[None, :], totals / tokens, jnp.zeros_like(totals))
    onehot = (node_map[0][:, None] == jnp.arange(HEADS)[None, :]).astype(jnp.float32)
    edge_scores = jnp.dot(onehot.T, raw_scores, precision=lax.Precision.HIGHEST)
    return (residual_grad[None], edge_scores[None])


def solution(mesh):
    placed = (
        P("section", None, "tp"),
        P("section", "tp", None),
        P("section", "tp", None),
        P("section", None, "tp"),
        P("section", "tp", None, None),
        P(),
        P("section", None),
    )
    return jax.shard_map(
        on_device,
        mesh=mesh,
        in_specs=placed,
        out_specs=(P("section", None, "tp"), P("section", None, None)),
        check_vma=False,
    )
```

profile of v0, /device:TPU:8, one launch (start us, length us, event | category | flops | bytes accessed | tf_op | source)
XLA Modules:
  0.0 441.4 jit_solution(2010720892174601740)
XLA Ops:
  7.2 0.0 copy-start
  7.2 0.0 all-gather.7.cloned.1.call-start
  7.2 0.7 all-gather.7.cloned.1.call-update
  7.9 6.4 %copy.21 = bf16[1,256,8192]{1,2,0:T(8,128)(2,1)} copy(bf16[1,256,8192]{2,1,0:T(8,128)(2,1)} %param.8) | data formatting | bytes 8388608 | tf_op args[1]
  14.3 0.0 copy-start.3
  14.3 8.6 %all-to-all-start = ((bf16[16,256,512]{1,2,0:T(8,128)(2,1)}), bf16[16,256,512]{1,2,0:T(8,128)(2,1)}, u32[]{:S(2)}, u32[]{:S(2)}) async-start(bf16[16,256,512]{1,2,0:T(8,128)(2,1)} %bitcast.55), calls=%async_computation | async-start | bytes 8388608 | tf_op jit(solution)/shard_map/all_to_all | solution.py:23
  23.0 0.0 all-gather.9.cloned.1.call-start
  23.0 0.7 all-gather.9.cloned.1.call-update
  23.7 0.0 all-gather.11.cloned.1.call-start
  23.8 0.0 copy-done.3
  23.8 0.1 and_convert_fusion
  24.0 0.0 copy-start.2
  24.0 0.0 copy-start.1
  24.0 125.0 %all-gather.7.cloned.1.call-done = bf16[1,160,8192]{2,1,0:T(8,128)(2,1)} async-done(((bf16[1,160,512]{2,1,0:T(8,128)(2,1)}), bf16[1,160,8192]{2,1,0:T(8,128)(2,1)}) %all-gather.7.cloned.1.call-update) | async-done | bytes 2621456 | tf_op jit(solution)/shard_map/all_gather | solution.py:33
  149.0 4.5 %fusion.14 = bf16[20,2,8,128]{3,2,1,0:T(8,128)(2,1)S(1)} fusion(bf16[1,256,8192]{2,1,0:T(8,128)(2,1)} %param.8, bf16[1,160,8192]{2,1,0:T(8,128)(2,1)} %all-gather.7.cloned.1.call-done), kind=kOutput, calls=%fused_computation.12 | convolution fusion | flops 671129600 | bytes 6897664 | tf_op jit(solution)/shard_map/dot_general | solution.py:34
  153.5 0.0 copy-done.2
  153.5 0.2 fusion.13
  153.8 2.7 dynamic_update_slice.3
  156.6 78.9 %all-reduce.1 = bf16[160,4,128]{2,1,0:T(4,128)(2,1)S(1)} all-reduce(f32[160,4,128]{2,1,0:T(4,128)S(1)} %dynamic_update_slice.3), channel_id=1, replica_groups=mesh['section'=32,'tp'=16] {'tp'}, use_global_device_ids=true, to_apply=%region_1.2 | all-reduce | flops 81920 | bytes 491520 | tf_op jit(solution)/shard_map/psum | solution.py:48
  235.5 0.0 copy-done
  235.5 0.0 copy-done.1
  235.5 1.0 fusion.41
  236.6 0.0 all-gather.11.cloned.1.call-update
  236.6 0.0 all-gather.9.cloned.1.call-done
  236.6 1.6 copy.29
  238.2 0.0 all-to-all-done
  238.2 6.4 %copy.22 = bf16[16,256,512]{2,1,0:T(8,128)(2,1)} copy(bf16[16,256,512]{1,2,0:T(8,128)(2,1)} %all-to-all-done) | data formatting | bytes 8388608 | tf_op jit(solution)/shard_map/all_to_all | solution.py:23
  244.6 6.0 %convolution_convert_fusion = bf16[32,160,512]{2,1,0:T(8,128)(2,1)} fusion(bf16[32,128,512]{2,1,0:T(8,128)(2,1)} %bitcast.56, bf16[160,32,128]{2,1,0:T(8,128)(2,1)S(1)} %bitcast.57), kind=kOutput, calls=%fused_computation.5 | convolution fusion | flops 673710080 | bytes 10747904 | tf_op jit(solution)/shard_map/thc,hcd->htd/dot_general | solution.py:56
  250.7 92.8 %all-gather.11.cloned.1.call-done = bf16[5120,512]{1,0:T(8,128)(2,1)} async-done(((bf16[160,512]{1,0:T(8,128)(2,1)}), bf16[5120,512]{1,0:T(8,128)(2,1)}) %all-gather.11.cloned.1.call-update) | async-done | bytes 5242896 | tf_op jit(solution)/shard_map/all_gather | solution.py:55
  343.5 0.0 copy-start.4
  343.5 15.0 %fusion.19 = f32[32,32]{1,0:T(8,128)S(1)} fusion(bf16[32,160,512]{2,1,0:T(8,128)(2,1)} %bitcast.61, bf16[32,160,512]{2,1,0:T(8,128)(2,1)} %convolution_convert_fusion), kind=kOutput, calls=%fused_computation.13 | convolution fusion | flops 167772160 | bytes 10489856 | tf_op jit(solution)/shard_map/dot_general | solution.py:62
  358.5 75.6 %psum.15 = f32[32,32]{1,0:T(8,128)S(1)} all-reduce(f32[32,32]{1,0:T(8,128)S(1)} %fusion.19), channel_id=1, replica_groups=mesh['section'=32,'tp'=16] {'tp'}, use_global_device_ids=true, to_apply=%region_2.3 | all-reduce | flops 1024 | bytes 8192 | tf_op jit(solution)/shard_map/psum | solution.py:68
  434.0 0.0 copy-done.4
  434.0 0.9 convolution_bitcast_fusion
  (4 shorter events, 0.1 us)
Async XLA Ops:
  7.2 228.3 %copy-start = (bf16[1,512,512]{2,1,0:T(8,128)(2,1)S(1)}, bf16[1,512,512]{2,1,0:T(8,128)(2,1)}, u32[]{:S(2)}) copy-start(bf16[1,512,512]{2,1,0:T(8,128)(2,1)} %param.9) | copy-start | bytes 1572868
  7.2 141.8 %all-gather.7.cloned.1.call-start = ((), (), s32[]{:S(2)}) async-start(), calls=%async_computation.1 | async-start | bytes 2785280 | tf_op jit(solution)/shard_map/all_gather | solution.py:33
  14.3 9.5 %copy-start.3 = (s32[160]{0:T(256)S(1)}, s32[160]{0:T(256)}, u32[]{:S(2)}) copy-start(s32[160]{0:T(256)} %param.12) | copy-start | bytes 1924
  14.3 223.9 %all-to-all-start = ((bf16[16,256,512]{1,2,0:T(8,128)(2,1)}), bf16[16,256,512]{1,2,0:T(8,128)(2,1)}, u32[]{:S(2)}, u32[]{:S(2)}) async-start(bf16[16,256,512]{1,2,0:T(8,128)(2,1)} %bitcast.55), calls=%async_computation | async-start | bytes 8388608 | tf_op jit(solution)/shard_map/all_to_all | solution.py:23
  23.0 213.6 %all-gather.9.cloned.1.call-start = ((), (), s32[]{:S(2)}) async-start(), calls=%async_computation.2 | async-start | bytes 1392640 | tf_op jit(solution)/shard_map/all_gather | solution.py:24
  23.7 319.7 %all-gather.11.cloned.1.call-start = ((), (), s32[]{:S(2)}) async-start(), calls=%async_computation.3 | async-start | bytes 5406720 | tf_op jit(solution)/shard_map/all_gather | solution.py:55
  24.0 129.5 %copy-start.2 = (bf16[1,2,160,160]{3,2,1,0:T(8,128)(2,1)S(1)}, bf16[1,2,160,160]{3,2,1,0:T(8,128)(2,1)}, u32[]{:S(2)}) copy-start(bf16[1,2,160,160]{3,2,1,0:T(8,128)(2,1)} %param.11) | copy-start | bytes 307204
  24.0 211.5 %copy-start.1 = (bf16[1,160,512]{2,1,0:T(8,128)(2,1)S(1)}, bf16[1,160,512]{2,1,0:T(8,128)(2,1)}, u32[]{:S(2)}) copy-start(bf16[1,160,512]{2,1,0:T(8,128)(2,1)} %param.7) | copy-start | bytes 491524
  343.5 90.5 %copy-start.4 = (s32[1,32]{1,0:T(1,128)S(1)}, s32[1,32]{1,0:T(1,128)}, u32[]{:S(2)}) copy-start(s32[1,32]{1,0:T(1,128)} %param.13) | copy-start | bytes 388
Sparse Core Ops, SparseCore 0:
  10.1 138.8 all-gather.6
  151.0 73.8 all-gather.8
  236.7 106.7 all-gather.10
where the time goes:
time: 442 us; the launch traced here: 441 us
  waiting for transfers between devices  219 us (50%)
  blocking collectives  154 us (35%)
  matrix products  27.7 us (6%)
  local copies, waits for them, and re-layouts  17.2 us (4%)
  between operations  13.9 us (3%)
  starting transfers between devices  8.77 us (2%)
    all_gather x1, waiting for transfers between devices, on_device(): grad_rows = lax.all_gather(grad_in[0], 'tp', axis=1, tiled=True)  125 us
    all_gather x1, waiting for transfers between devices, on_device(): lax.all_gather(target_row[None], 'section', axis=0, tiled=True)  92.8 us
    psum x1, blocking collectives, on_device(): summed = lax.psum(slots, 'tp')  78.9 us
    psum x1, blocking collectives, on_device(): totals = lax.psum(partial_scores, 'tp')  75.6 us
    dot_general x1, matrix products, on_device(): lax.dot_general(delta.reshape(HEADS, tokens * local_width), target_rows.r...  15 us
  transfers between devices with their start and end apart: 4, of which 2 were waited for; matrix products, arithmetic and copies ran while one was open for 7% of the time, Pallas kernels for 0%

commit v1 on v0

--- a/solution.py
+++ b/solution.py
@@ -45,7 +45,7 @@
     group_of = lax.axis_index("tp") * own_heads // GROUP
     slots = jnp.zeros((tokens, KV, HEAD_DIM), jnp.float32)
     slots = lax.dynamic_update_slice(slots, pair_sum[:, None, :], (0, group_of, 0))
-    summed = lax.psum(slots, "tp")
+    summed = jnp.sum(lax.all_gather(slots, "tp"), axis=0)
     group_grad = summed.reshape(tokens, KV * HEAD_DIM).astype(jnp.bfloat16)
     increment = lax.dot_general(
         group_grad, value_proj[0], (((1,), (1,)), ((), ())), preferred_element_type=jnp.float32

time: 442 us -> 549 us (1.24)
  waiting for transfers between devices: 219 us -> 405 us
  blocking collectives: 154 us -> 75.6 us
    all_gather x0 -> x1, waiting for transfers between devices: none -> 121 us  [on_device(): summed = jnp.sum(lax.all_gather(slots, 'tp'), axis=0)]
    all_gather x1, waiting for transfers between devices: 0.02 us -> 90.8 us  [on_device(): all_delta_cols = lax.all_gather(head_delta[0], 'tp', axis=1, tiled=True)]
    psum x1 -> x0, blocking collectives: 78.9 us -> none  [on_device(): summed = lax.psum(slots, 'tp')]
    all_gather x1, waiting for transfers between devices: 125 us -> 95.2 us  [on_device(): grad_rows = lax.all_gather(grad_in[0], 'tp', axis=1, tiled=True)]
  transfers between devices with their start and end apart: 4 -> 5, of which waited for: 2 -> 4; matrix products, arithmetic and copies ran while one was open for 7% -> 5% of each run, Pallas kernels for 0% -> 0%
where the time goes in v1:
time: 549 us; the launch traced here: 548 us
  waiting for transfers between devices  405 us (74%)
  blocking collectives  75.6 us (14%)
  matrix products  27.7 us (5%)
  local copies, waits for them, and re-layouts  15.2 us (3%)
  between operations  13.9 us (3%)
  starting transfers between devices  6.5 us (1%)
    all_gather x1, waiting for transfers between devices, on_device(): summed = jnp.sum(lax.all_gather(slots, 'tp'), axis=0)  121 us
    all_gather x1, waiting for transfers between devices, on_device(): lax.all_gather(target_row[None], 'section', axis=0, tiled=True)  96.5 us
    all_gather x1, waiting for transfers between devices, on_device(): grad_rows = lax.all_gather(grad_in[0], 'tp', axis=1, tiled=True)  95.2 us
    all_gather x1, waiting for transfers between devices, on_device(): all_delta_cols = lax.all_gather(head_delta[0], 'tp', axis=1, tiled=True)  90.8 us
    psum x1, blocking collectives, on_device(): totals = lax.psum(partial_scores, 'tp')  75.6 us
    dot_general x1, matrix products, on_device(): lax.dot_general(delta.reshape(HEADS, tokens * local_width), target_rows.r...  15 us
  transfers between devices with their start and end apart: 5, of which 4 were waited for; matrix products, arithmetic and copies ran while one was open for 5% of the time, Pallas kernels for 0%

profile of v1, /device:TPU:8, one launch (start us, length us, event | category | flops | bytes accessed | tf_op | source)
XLA Modules:
  0.0 548.5 jit_solution(14516808069639608405)
XLA Ops:
  7.2 0.0 copy-start
  7.2 0.0 all-gather.10.cloned.1.call-start
  7.2 0.7 all-gather.10.cloned.1.call-update
  7.9 0.0 all-gather.8.cloned.1.call-start
  8.0 0.7 broadcast_compare_fusion
  8.7 0.9 and_convert_fusion
  9.6 0.0 copy-start.3
  9.6 95.2 %all-gather.10.cloned.1.call-done = bf16[1,160,8192]{2,1,0:T(8,128)(2,1)} async-done(((bf16[1,160,512]{2,1,0:T(8,128)(2,1)}), bf16[1,160,8192]{2,1,0:T(8,128)(2,1)}) %all-gather.10.cloned.1.call-update) | async-done | bytes 2621456 | tf_op jit(solution)/shard_map/all_gather | solution.py:33
  104.7 4.5 fusion.14
  109.3 0.0 copy-done.3
  109.3 0.2 fusion.13
  109.6 0.0 copy-start.1
  109.6 0.7 copy-done.1
  110.3 0.0 all-gather.8.cloned.1.call-update
  110.3 6.4 %copy.43 = bf16[1,256,8192]{1,2,0:T(8,128)(2,1)} copy(bf16[1,256,8192]{2,1,0:T(8,128)(2,1)} %param.8) | data formatting | bytes 8388608 | tf_op args[1]
  116.8 6.3 %all-to-all-start = ((bf16[16,256,512]{1,2,0:T(8,128)(2,1)}), bf16[16,256,512]{1,2,0:T(8,128)(2,1)}, u32[]{:S(2)}, u32[]{:S(2)}) async-start(bf16[16,256,512]{1,2,0:T(8,128)(2,1)} %bitcast.61), calls=%async_computation | async-start | bytes 8388608 | tf_op jit(solution)/shard_map/all_to_all | solution.py:23
  123.1 0.0 copy-start.2
  123.1 0.0 all-gather.12.cloned.1.call-start
  123.2 0.7 all-gather.12.cloned.1.call-update
  123.9 0.0 all-gather.14.cloned.1.call-start
  123.9 121.4 %all-gather.8.cloned.1.call-done = f32[16,160,4,128]{3,1,2,0:T(8,128)} async-done(((f32[1,160,4,128]{3,1,2,0:T(8,128)}), f32[16,160,4,128]{3,1,2,0:T(8,128)}) %all-gather.8.cloned.1.call-update) | async-done | bytes 5242896 | tf_op jit(solution)/shard_map/all_gather | solution.py:48
  245.3 2.8 reduce_sum.22
  248.0 0.0 copy-done
  248.1 0.0 copy-done.2
  248.1 1.0 fusion.41
  249.1 0.0 all-gather.14.cloned.1.call-update
  249.2 90.8 %all-gather.12.cloned.1.call-done = bf16[1,160,4096]{2,1,0:T(8,128)(2,1)} async-done(((bf16[1,160,256]{2,1,0:T(8,128)(2,1)}), bf16[1,160,4096]{2,1,0:T(8,128)(2,1)}) %all-gather.12.cloned.1.call-update) | async-done | bytes 1310736 | tf_op jit(solution)/shard_map/all_gather | solution.py:24
  340.0 1.6 copy.51
  341.6 0.0 all-to-all-done
  341.6 6.4 %copy.44 = bf16[16,256,512]{2,1,0:T(8,128)(2,1)} copy(bf16[16,256,512]{1,2,0:T(8,128)(2,1)} %all-to-all-done) | data formatting | bytes 8388608 | tf_op jit(solution)/shard_map/all_to_all | solution.py:23
  348.0 6.1 %convolution_convert_fusion = bf16[32,160,512]{2,1,0:T(8,128)(2,1)} fusion(bf16[32,128,512]{2,1,0:T(8,128)(2,1)} %bitcast.62, bf16[160,32,128]{2,1,0:T(8,128)(2,1)S(1)} %bitcast.63), kind=kOutput, calls=%fused_computation.5 | convolution fusion | flops 673710080 | bytes 10747904 | tf_op jit(solution)/shard_map/thc,hcd->htd/dot_general | solution.py:56
  354.1 96.5 %all-gather.14.cloned.1.call-done = bf16[5120,512]{1,0:T(8,128)(2,1)} async-done(((bf16[160,512]{1,0:T(8,128)(2,1)}), bf16[5120,512]{1,0:T(8,128)(2,1)}) %all-gather.14.cloned.1.call-update) | async-done | bytes 5242896 | tf_op jit(solution)/shard_map/all_gather | solution.py:55
  450.6 0.0 copy-start.4
  450.6 15.0 %fusion.19 = f32[32,32]{1,0:T(8,128)S(1)} fusion(bf16[32,160,512]{2,1,0:T(8,128)(2,1)} %bitcast.65, bf16[32,160,512]{2,1,0:T(8,128)(2,1)} %convolution_convert_fusion), kind=kOutput, calls=%fused_computation.13 | convolution fusion | flops 167772160 | bytes 10489856 | tf_op jit(solution)/shard_map/dot_general | solution.py:62
  465.5 75.6 %psum.7 = f32[32,32]{1,0:T(8,128)S(1)} all-reduce(f32[32,32]{1,0:T(8,128)S(1)} %fusion.19), channel_id=1, replica_groups=mesh['section'=32,'tp'=16] {'tp'}, use_global_device_ids=true, to_apply=%region_2.3 | all-reduce | flops 1024 | bytes 8192 | tf_op jit(solution)/shard_map/psum | solution.py:68
  541.1 0.0 copy-done.4
  541.1 0.9 convolution_bitcast_fusion
  (4 shorter events, 0.0 us)
Async XLA Ops:
  7.2 240.9 %copy-start = (bf16[1,512,512]{2,1,0:T(8,128)(2,1)S(1)}, bf16[1,512,512]{2,1,0:T(8,128)(2,1)}, u32[]{:S(2)}) copy-start(bf16[1,512,512]{2,1,0:T(8,128)(2,1)} %param.9) | copy-start | bytes 1572868
  7.2 97.6 %all-gather.10.cloned.1.call-start = ((), (), s32[]{:S(2)}) async-start(), calls=%async_computation.2 | async-start | bytes 2785280 | tf_op jit(solution)/shard_map/all_gather | solution.py:33
  7.9 237.3 %all-gather.8.cloned.1.call-start = ((), (), s32[]{:S(2)}) async-start(), calls=%async_computation.1 | async-start | bytes 5570560 | tf_op jit(solution)/shard_map/all_gather | solution.py:48
  9.6 99.7 %copy-start.3 = (bf16[1,2,160,160]{3,2,1,0:T(8,128)(2,1)S(1)}, bf16[1,2,160,160]{3,2,1,0:T(8,128)(2,1)}, u32[]{:S(2)}) copy-start(bf16[1,2,160,160]{3,2,1,0:T(8,128)(2,1)} %param.11) | copy-start | bytes 307204
  109.6 0.7 copy-start.1
  116.8 224.8 %all-to-all-start = ((bf16[16,256,512]{1,2,0:T(8,128)(2,1)}), bf16[16,256,512]{1,2,0:T(8,128)(2,1)}, u32[]{:S(2)}, u32[]{:S(2)}) async-start(bf16[16,256,512]{1,2,0:T(8,128)(2,1)} %bitcast.61), calls=%async_computation | async-start | bytes 8388608 | tf_op jit(solution)/shard_map/all_to_all | solution.py:23
  123.1 125.0 %copy-start.2 = (bf16[1,160,512]{2,1,0:T(8,128)(2,1)S(1)}, bf16[1,160,512]{2,1,0:T(8,128)(2,1)}, u32[]{:S(2)}) copy-start(bf16[1,160,512]{2,1,0:T(8,128)(2,1)} %param.7) | copy-start | bytes 491524
  123.1 216.9 %all-gather.12.cloned.1.call-start = ((), (), s32[]{:S(2)}) async-start(), calls=%async_computation.3 | async-start | bytes 1392640 | tf_op jit(solution)/shard_map/all_gather | solution.py:24
  123.9 326.7 %all-gather.14.cloned.1.call-start = ((), (), s32[]{:S(2)}) async-start(), calls=%async_computation.4 | async-start | bytes 5406720 | tf_op jit(solution)/shard_map/all_gather | solution.py:55
  450.6 90.5 %copy-start.4 = (s32[1,32]{1,0:T(1,128)S(1)}, s32[1,32]{1,0:T(1,128)}, u32[]{:S(2)}) copy-start(s32[1,32]{1,0:T(1,128)} %param.13) | copy-start | bytes 388
Sparse Core Ops, SparseCore 0:
  10.1 94.5 all-gather.9
  110.5 134.7 all-gather.7
  247.3 92.6 all-gather.11
  343.0 107.5 all-gather.13
